TPU v7x, 256 devices: a whole 4x4x8 slice. The times are simulated.
256 devices in a mesh: kv: 8 (over y, z_lo), blk: 32 (over x, z_hi, core).
Axes of the slice: x: 4, y: 4, z: 8 (z_hi: 4, z_lo: 2; z = z_hi * 2 + z_lo), core: 2. Of those that a mesh axis runs over, the one named last changes fastest.
Arguments:
- suffix_query: bfloat16 [6144, 4096], P('blk', 'kv'), may hold values from -6 to 6
- suffix_key_value: bfloat16 [2, 6144, 2048], P(None, 'blk', 'kv'), may hold values from -6 to 6
- suffix_resid: bfloat16 [6144, 4608], P('blk', 'kv'), may hold values from -6 to 6
- decode_query_rows: bfloat16 [64, 4096], P('blk', 'kv'), may hold values from -6 to 6
- decode_key_value: bfloat16 [2, 64, 2048], P(None, 'blk', 'kv'), may hold values from -6 to 6
- decode_resid: bfloat16 [64, 4608], P('blk', 'kv'), may hold values from -6 to 6
- out_weight: bfloat16 [4096, 4608], P('kv'), may hold values from -1.125 to 1.125
- post_gain: float32 [4608], P('kv'), may hold values from 0.1 to 1.9
- prefix_page_store: bfloat16 [2, 96, 128, 2048], P(None, 'blk', None, 'kv'), may hold values from -6 to 6
- prefix_table: int32 [96], replicated, may hold values from 0 to 95, each once
- decode_page_store: bfloat16 [2, 512, 128, 2048], P(None, 'blk', None, 'kv'), may hold values from -6 to 6
- page_table: int32 [512], replicated, may hold values from 0 to 511, each once
- suffix_lengths: int32 [16], replicated, may hold values from 1 to 768, 6144 in all
- suffix_prefix: int32 [16], replicated, may hold values from 0 to 3
- decode_ages: int32 [64], replicated, may hold values from 1 to 1023, as said below
Outputs:
- suffix_hidden: bfloat16 [6144, 4608], P('blk', 'kv')
- decode_hidden: bfloat16 [64, 4608], P('blk', 'kv')
- new_cache: bfloat16 [2, 512, 128, 2048], P(None, 'blk', None, 'kv')
Inputs may be any that keep to these rules, and one draw needn't show every extreme that they name: `page_table`: every page of the decode pool is named once. `prefix_table`: every page of the prefix pool is named once. `suffix_lengths`: the lengths sum to 6144; one is exactly 768. `decode_ages`: some slot has age 1024 - 1.
All inputs are finite; a program needn't handle non-finite values.
Results may differ from a plain program's by a relative error of at most 0.024.
Values may be sent and summed in bfloat16 or wider, within the bound.
No kernel may reach another device: no remote copies, remote signals or barrier semaphores. Data moves between devices by JAX's collectives and lax.ppermute only.
A program may use at most 128 MiB of HBM per device.

v0:
```python
import math
import jax
import jax.numpy as jnp
from jax import lax
from jax.sharding import PartitionSpec as P

D = 4608
QUERY_HEADS = 32
HEAD_SIZE = 128
PAGE_TOKENS = 128
PREFIX_LENGTH = 3072
SLOT_CAPACITY = 1024
soft_cap = 50.0
norm_eps = 1e-06


def from_behind(block, axis, distance):
    devices = range(lax.axis_size(axis))
    route = [(i - distance, i) for i in devices if i - distance in devices]
    return lax.ppermute(block, axis, route)


def attend(query_rows, key_rows, value_rows, visible, q_scale):
    logits = (
        jnp.einsum("qhgd,khd->qhgk", query_rows, key_rows, preferred_element_type=jnp.float32)
        * q_scale
    )
    capped = soft_cap * jnp.tanh(logits / soft_cap)
    weights = jnp.where(visible[:, None, None, :], jnp.exp(capped), 0.0)
    denominator = jnp.sum(weights, axis=3)
    numerator = jnp.einsum(
        "qhgk,khd->qhgd",
        weights.astype(jnp.bfloat16),
        value_rows,
        preferred_element_type=jnp.float32,
    )
    return (numerator, denominator)


def earlier(block_rows):
    return from_behind(block_rows, "blk", 1)


def token_tables(lengths, prefix_ids, token_ids):
    suffix_ends = jnp.cumsum(lengths)
    starts = suffix_ends - lengths
    inside = (
        (token_ids[:, None] >= starts[None, :]) & (token_ids[:, None] < suffix_ends[None, :])
    ).astype(jnp.int32)
    tok_start = jnp.sum(inside * starts[None, :], axis=1)
    tok_prefix = jnp.sum(inside * prefix_ids[None, :], axis=1)
    return (tok_start, tok_prefix)


def inverse_rows(table, wanted):
    hits = (table[None, :] == wanted[:, None]).astype(jnp.int32)
    places = jnp.arange(table.shape[0], dtype=jnp.int32)
    return jnp.sum(hits * places[None, :], axis=1)


def body(
    suffix_query,
    suffix_key_value,
    suffix_resid,
    decode_query_rows,
    decode_key_value,
    decode_resid,
    out_weight,
    post_gain,
    prefix_page_store,
    prefix_table,
    decode_page_store,
    page_table,
    suffix_lengths,
    suffix_prefix,
    decode_ages,
):
    head_dim = HEAD_SIZE
    page_len = PAGE_TOKENS
    q_scale = (D // QUERY_HEADS) ** (-0.5)
    tok_rows = suffix_query.shape[0]
    q_heads = suffix_query.shape[1] // head_dim
    kv_heads = suffix_key_value.shape[2] // head_dim
    query_group_width = q_heads // kv_heads
    my_index = lax.axis_index("blk")
    own_queries = suffix_query.reshape(tok_rows, kv_heads, query_group_width, head_dim)
    token_ids = my_index * tok_rows + jnp.arange(tok_rows, dtype=jnp.int32)
    tok_start, tok_prefix = token_tables(suffix_lengths, suffix_prefix, token_ids)
    look_back = 4
    pieces_back = [suffix_key_value]
    for step in range(look_back):
        pieces_back.insert(0, earlier(pieces_back[0]))
    window = jnp.concatenate(pieces_back, axis=1)
    key_ids = (my_index - look_back) * tok_rows + jnp.arange(
        (look_back + 1) * tok_rows, dtype=jnp.int32
    )
    visible = (key_ids[None, :] >= tok_start[:, None]) & (key_ids[None, :] <= token_ids[:, None])
    window_keys = window[0].reshape((look_back + 1) * tok_rows, kv_heads, head_dim)
    window_values = window[1].reshape((look_back + 1) * tok_rows, kv_heads, head_dim)
    own_numer, own_denom = attend(own_queries, window_keys, window_values, visible, q_scale)
    pool_pages = prefix_table.shape[0]
    page_owner = inverse_rows(prefix_table, jnp.arange(pool_pages, dtype=jnp.int32)) // (
        PREFIX_LENGTH // PAGE_TOKENS
    )
    all_queries = lax.all_gather(suffix_query, "blk", axis=0, tiled=True)
    all_tokens = all_queries.shape[0]
    all_ids = jnp.arange(all_tokens, dtype=jnp.int32)
    unused_start, all_prefix = token_tables(suffix_lengths, suffix_prefix, all_ids)
    local_pages = prefix_page_store.shape[1]
    held_owner = lax.dynamic_slice_in_dim(page_owner, my_index * local_pages, local_pages, 0)
    held_cols = jnp.repeat(held_owner, page_len)
    held_keys = prefix_page_store[0].reshape(local_pages * page_len, kv_heads, head_dim)
    held_values = prefix_page_store[1].reshape(local_pages * page_len, kv_heads, head_dim)
    block_rows = math.gcd(all_tokens, 1024)
    query_blocks = all_queries.reshape(
        all_tokens // block_rows, block_rows, kv_heads, query_group_width, head_dim
    )
    prefix_blocks = all_prefix.reshape(all_tokens // block_rows, block_rows)

    def one_block(element):
        block_queries, block_prefix = element
        seen = block_prefix[:, None] == held_cols[None, :]
        return attend(block_queries, held_keys, held_values, seen, q_scale)

    numer_all, denom_all = lax.map(one_block, (query_blocks, prefix_blocks))
    numer_all = numer_all.reshape(all_tokens, kv_heads, query_group_width, head_dim)
    denom_all = denom_all.reshape(all_tokens, kv_heads, query_group_width)
    pre_numer, pre_denom = (
        lax.psum_scatter(
            numer_all.astype(jnp.bfloat16), "blk", scatter_dimension=0, tiled=True
        ).astype(jnp.float32),
        lax.psum_scatter(
            denom_all.astype(jnp.bfloat16), "blk", scatter_dimension=0, tiled=True
        ).astype(jnp.float32),
    )
    suffix_attn = ((own_numer + pre_numer) / (own_denom + pre_denom)[..., None]).astype(
        jnp.bfloat16
    )
    suffix_attn = suffix_attn.reshape(tok_rows, q_heads * head_dim)
    all_dq, all_dkv = (
        lax.all_gather(decode_query_rows, "blk", axis=0, tiled=True),
        lax.all_gather(decode_key_value, "blk", axis=1, tiled=True),
    )
    slot_total = all_dq.shape[0]
    slot_pages = SLOT_CAPACITY // PAGE_TOKENS
    local_cache = decode_page_store.shape[1]
    page_ids = my_index * local_cache + jnp.arange(local_cache, dtype=jnp.int32)
    position = inverse_rows(page_table, page_ids)
    slot_of = position // slot_pages
    block_of = position % slot_pages
    slot_hot = slot_of[:, None] == jnp.arange(slot_total, dtype=jnp.int32)[None, :]
    page_age = jnp.sum(slot_hot.astype(jnp.int32) * decode_ages[None, :], axis=1)
    select = slot_hot.astype(jnp.bfloat16)
    new_rows = jnp.einsum(
        "ls,tsc->tlc", select, all_dkv, preferred_element_type=jnp.float32
    ).astype(jnp.bfloat16)
    write_here = (block_of == page_age // page_len)[:, None] & (
        jnp.arange(page_len, dtype=jnp.int32)[None, :] == (page_age % page_len)[:, None]
    )
    new_cache = jnp.where(write_here[None, :, :, None], new_rows[:, :, None, :], decode_page_store)
    page_queries = jnp.dot(select, all_dq, preferred_element_type=jnp.float32).astype(jnp.bfloat16)
    page_queries = page_queries.reshape(local_cache, kv_heads, query_group_width, head_dim)
    key_cache = new_cache[0].reshape(local_cache, page_len, kv_heads, head_dim)
    value_cache = new_cache[1].reshape(local_cache, page_len, kv_heads, head_dim)
    logits = (
        jnp.einsum("lhgd,lphd->lhgp", page_queries, key_cache, preferred_element_type=jnp.float32)
        * q_scale
    )
    capped = soft_cap * jnp.tanh(logits / soft_cap)
    places = block_of[:, None] * page_len + jnp.arange(page_len, dtype=jnp.int32)[None, :]
    seen_pos = places <= page_age[:, None]
    weights = jnp.where(seen_pos[:, None, None, :], jnp.exp(capped), 0.0)
    page_denom = jnp.sum(weights, axis=3)
    page_numer = jnp.einsum(
        "lhgp,lphd->lhgd",
        weights.astype(jnp.bfloat16),
        value_cache,
        preferred_element_type=jnp.float32,
    )
    slot_float = slot_hot.astype(jnp.float32)
    slot_numer = jnp.einsum(
        "ls,lhgd->shgd", slot_float, page_numer, precision=lax.Precision.HIGHEST
    )
    slot_denom = jnp.einsum("ls,lhg->shg", slot_float, page_denom, precision=lax.Precision.HIGHEST)
    mine_numer, mine_denom = (
        lax.psum_scatter(
            slot_numer.astype(jnp.bfloat16), "blk", scatter_dimension=0, tiled=True
        ).astype(jnp.float32),
        lax.psum_scatter(
            slot_denom.astype(jnp.bfloat16), "blk", scatter_dimension=0, tiled=True
        ).astype(jnp.float32),
    )
    decode_attn = (mine_numer / mine_denom[..., None]).astype(jnp.bfloat16)
    decode_rows = decode_attn.shape[0]
    decode_attn = decode_attn.reshape(decode_rows, q_heads * head_dim)
    attention = jnp.concatenate([suffix_attn, decode_attn], axis=0)
    projected = jnp.dot(attention, out_weight, preferred_element_type=jnp.float32)
    residual = jnp.concatenate([suffix_resid, decode_resid], axis=0).astype(jnp.float32)
    mine = lax.psum_scatter(
        projected.astype(jnp.bfloat16), "kv", scatter_dimension=1, tiled=True
    ).astype(jnp.float32)
    mean_square = lax.psum(jnp.sum(mine * mine, axis=1), "kv") / D
    normed = mine * lax.rsqrt(mean_square + norm_eps)[:, None] * post_gain[None, :]
    hidden = (residual + normed).astype(jnp.bfloat16)
    return (hidden[:tok_rows], hidden[tok_rows:], new_cache)


def solution(mesh):
    placed = (
        P("blk", "kv"),
        P(None, "blk", "kv"),
        P("blk", "kv"),
        P("blk", "kv"),
        P(None, "blk", "kv"),
        P("blk", "kv"),
        P("kv", None),
        P("kv"),
        P(None, "blk", None, "kv"),
        P(),
        P(None, "blk", None, "kv"),
        P(),
        P(),
        P(),
        P(),
    )
    return jax.shard_map(
        body,
        mesh=mesh,
        in_specs=placed,
        out_specs=(P("blk", "kv"), P("blk", "kv"), P(None, "blk", None, "kv")),
        check_vma=False,
    )
```

profile of v0, /device:TPU:2, one launch (start us, length us, event | category | flops | bytes accessed | tf_op | source)
XLA Modules:
  0.0 656.7 jit_solution(15037850193555876869)
XLA Ops:
  8.7 3.9 copy.90
  12.6 42.1 %all-gather = bf16[32,2,512]{2,1,0:T(2,128)(2,1)S(1)} all-gather(bf16[1,2,512]{2,1,0:T(2,128)(2,1)S(1)} %bitcast.118), channel_id=1, replica_groups=mesh['kv'=8,'blk'=32] {'blk'}, dimensions={0}, use_global_device_ids=true | all-gather | bytes 67584 | tf_op jit(solution)/shard_map/all_gather | solution.py:141
  55.2 42.4 %all_gather.11 = bf16[2,64,256]{2,0,1:T(2,128)(2,1)S(1)} all-gather(bf16[2,2,256]{2,0,1:T(2,128)(2,1)S(1)} %copy.88), channel_id=1, replica_groups=mesh['kv'=8,'blk'=32] {'blk'}, dimensions={1}, use_global_device_ids=true | all-gather | bytes 67584 | tf_op jit(solution)/shard_map/all_gather | solution.py:142
  103.9 9.7 %reshape.292 = bf16[6,1024,2,2,128]{4,3,2,1,0:T(2,128)(2,1)} reshape(bf16[6144,512]{1,0:T(8,128)(2,1)} %all-gather.3.cloned.1.call-done) | data formatting | bytes 12582912 | tf_op jit(solution)/shard_map/reshape | solution.py:115
  113.6 49.5 %while.15 = (s32[]{:T(128)}, bf16[6,1024,2,2,128]{4,1,3,2,0:T(8,128)(2,1)}, bf16[6,1024,2,2]{1,3,2,0:T(2,128)(2,1)S(1)}, s32[6,1024]{1,0:T(8,128)S(1)}, bf16[6,1...) while((s32[]{:T(128)}, ...), condition=%wide.region_6.7_spmd.clone, body=%wide.region_4.6_spmd.clone.sunk | while | flops 818278400 | bytes 19439220 | solution.py:125
  118.6 3.2 bitcast_dynamic-update-slice_fusion.4
  135.1 3.2 bitcast_dynamic-update-slice_fusion.4
  143.3 3.2 bitcast_dynamic-update-slice_fusion.4
  151.6 3.2 bitcast_dynamic-update-slice_fusion.4
  159.8 3.2 bitcast_dynamic-update-slice_fusion.4
  163.1 5.8 copy.117
  168.9 6.3 reshape.304
  175.2 6.1 copy.85
  186.0 125.5 %all-reduce.1 = bf16[64,2,2]{2,0,1:T(8,128)(2,1)S(1)} all-reduce(bf16[64,2,2]{2,0,1:T(8,128)(2,1)S(1)} %convolution_convert_fusion.2), channel_id=5, replica_groups=mesh['kv'=8,'blk'=32] {'blk'}, use_global_device_ids=true, to_apply=%region_14.15.clone | all-reduce | flops 256 | bytes 1024
  313.7 8.1 %collective-permute-done.1 = bf16[2,192,256]{2,1,0:T(8,128)(2,1)S(1)} collective-permute-done((bf16[2,192,256]{2,1,0:T(8,128)(2,1)S(1)}, bf16[2,192,256]{2,1,0:T(8,128)(2,1)S(1)}, u32[]{:S(2)}, u32[]{:S(2)}) %collective-permute-start.1) | collective-permute-done | bytes 196640 | tf_op jit(solution)/shard_map/ppermute | solution.py:20
  323.9 7.8 %collective-permute-done.2 = bf16[2,192,256]{2,1,0:T(8,128)(2,1)S(1)} collective-permute-done((bf16[2,192,256]{2,1,0:T(8,128)(2,1)S(1)}, bf16[2,192,256]{2,1,0:T(8,128)(2,1)S(1)}, u32[]{:S(2)}, u32[]{:S(2)}) %collective-permute-start.2) | collective-permute-done | bytes 196640 | tf_op jit(solution)/shard_map/ppermute | solution.py:20
  333.9 9.5 %all-reduce.4.cloned.1.call-done = bf16[64,2,2,128]{3,0,2,1:T(8,128)(2,1)} async-done(((bf16[64,2,2,128]{3,0,2,1:T(8,128)(2,1)}), bf16[64,2,2,128]{3,0,2,1:T(8,128)(2,1)}) %all-reduce.4.cloned.1.call-update) | async-done | bytes 65552
  345.4 3.9 fusion.10
  349.2 99.7 %reduce-scatter.12.cloned.1.call-done = bf16[192,4]{1,0:T(8,128)(2,1)} async-done(((bf16[6144,4]{1,0:T(8,128)(2,1)}), bf16[192,4]{1,0:T(8,128)(2,1)}) %reduce-scatter.12.cloned.1.call-update) | async-done | bytes 1552
  449.9 109.7 %reduce-scatter.10.cloned.1.call-done = bf16[192,2,2,128]{3,0,2,1:T(8,128)(2,1)} async-done(((bf16[6144,2,2,128]{3,0,2,1:T(8,128)(2,1)}), bf16[192,2,2,128]{3,0,2,1:T(8,128)(2,1)}) %reduce-scatter.10.cloned.1.call-update) | async-done | bytes 196624 | tf_op jit(solution)/shard_map/reduce_scatter | solution.py:129
  562.8 4.7 convolution_convert_fusion
  567.5 4.0 copy.115
  574.2 56.4 %reduce-scatter.14.cloned.1.call-done = bf16[576,194]{1,0:T(8,128)(2,1)} async-done(((bf16[4608,194]{1,0:T(8,128)(2,1)}), bf16[576,194]{1,0:T(8,128)(2,1)}) %reduce-scatter.14.cloned.1.call-update) | async-done | bytes 223504
  631.8 16.9 %psum.7 = f32[194]{0:T(256)S(1)} all-reduce(f32[194]{0:T(256)S(1)} %fusion.32), channel_id=1, replica_groups=mesh['kv'=8,'blk'=32] {'kv'}, use_global_device_ids=true, to_apply=%region_17.18 | all-reduce | flops 194 | bytes 1552 | tf_op jit(solution)/shard_map/psum | solution.py:202
  (146 shorter events, 63.3 us)
Async XLA Ops:
  7.2 5.4 copy-start.6
  7.2 47.6 %copy-start.7 = (s32[512]{0:T(512)S(1)}, s32[512]{0:T(512)}, u32[]{:S(2)}) copy-start(s32[512]{0:T(512)} %param.28) | copy-start | bytes 6148
  7.2 90.3 %copy-start.10 = (s32[64]{0:T(128)S(1)}, s32[64]{0:T(128)}, u32[]{:S(2)}) copy-start(s32[64]{0:T(128)} %param.31) | copy-start | bytes 772
  7.2 96.7 %all-gather.3.cloned.1.call-start = ((), (), s32[]{:S(2)}) async-start(), calls=%async_computation.3 | async-start | bytes 6488064 | tf_op jit(solution)/shard_map/all_gather | solution.py:105
  7.9 335.4 %all-reduce.4.cloned.1.call-start = ((), (), s32[]{:S(2)}) async-start(), calls=%async_computation.7 | async-start | bytes 131072
  100.6 2.4 copy-start.11
  100.6 2.5 copy-start.8
  100.6 2.8 copy-start.9
  100.6 3.0 copy-start.1
  102.9 346.0 %reduce-scatter.12.cloned.1.call-start = ((), (), s32[]{:S(2)}) async-start(), calls=%async_computation.5 | async-start | bytes 1622016
  175.1 384.5 %reduce-scatter.10.cloned.1.call-start = ((), (), s32[]{:S(2)}) async-start(), calls=%async_computation.4 | async-start | bytes 6488064 | tf_op jit(solution)/shard_map/reduce_scatter | solution.py:129
  181.2 0.9 copy-start.3
  181.2 3.2 copy-start
  181.2 3.3 copy-start.12
  181.3 449.3 %reduce-scatter.14.cloned.1.call-start = ((), (), s32[]{:S(2)}) async-start(), calls=%async_computation.6 | async-start | bytes 2654208
  182.2 129.5 %collective-permute-start = (bf16[2,192,256]{2,1,0:T(8,128)(2,1)S(1)}, bf16[2,192,256]{2,1,0:T(8,128)(2,1)S(1)}, u32[]{:S(2)}, u32[]{:S(2)}) collective-permute-start(bf16[2,192,256]{2,1,0:T(8,128)(2,1)S(1)} %copy-done.3), channel_id=1, source_target_pairs={{0,1},{1,2},{2,3},{3,4},{4,5},{5,6},{6,7},{7,8},{8,9},{9,10},{10,1... | collective-permute-start | bytes 589832 | tf_op jit(solution)/shard_map/ppermute | solution.py:20
  311.7 10.1 %collective-permute-start.1 = (bf16[2,192,256]{2,1,0:T(8,128)(2,1)S(1)}, bf16[2,192,256]{2,1,0:T(8,128)(2,1)S(1)}, u32[]{:S(2)}, u32[]{:S(2)}) collective-permute-start(bf16[2,192,256]{2,1,0:T(8,128)(2,1)S(1)} %collective-permute-done), channel_id=1, source_target_pairs={{0,1},{1,2},{2,3},{3,4},{4,5},{5,6},{6,7},{7,8},{8,9},{9,10},{10,1... | collective-permute-start | bytes 589832 | tf_op jit(solution)/shard_map/ppermute | solution.py:20
  321.8 10.0 %collective-permute-start.2 = (bf16[2,192,256]{2,1,0:T(8,128)(2,1)S(1)}, bf16[2,192,256]{2,1,0:T(8,128)(2,1)S(1)}, u32[]{:S(2)}, u32[]{:S(2)}) collective-permute-start(bf16[2,192,256]{2,1,0:T(8,128)(2,1)S(1)} %collective-permute-done.1), channel_id=1, source_target_pairs={{0,1},{1,2},{2,3},{3,4},{4,5},{5,6},{6,7},{7,8},{8,9},{9,10},{10,1... | collective-permute-start | bytes 589832 | tf_op jit(solution)/shard_map/ppermute | solution.py:20
  331.8 12.4 %collective-permute-start.3 = (bf16[2,192,256]{2,1,0:T(8,128)(2,1)S(1)}, bf16[2,192,256]{2,1,0:T(8,128)(2,1)S(1)}, u32[]{:S(2)}, u32[]{:S(2)}) collective-permute-start(bf16[2,192,256]{2,1,0:T(8,128)(2,1)S(1)} %collective-permute-done.2), channel_id=1, source_target_pairs={{0,1},{1,2},{2,3},{3,4},{4,5},{5,6},{6,7},{7,8},{8,9},{9,10},{10,1... | collective-permute-start | bytes 589832 | tf_op jit(solution)/shard_map/ppermute | solution.py:20
  571.5 77.2 %copy-start.2 = (bf16[192,576]{1,0:T(8,128)(2,1)S(1)}, bf16[192,576]{1,0:T(8,128)(2,1)}, u32[]{:S(2)}) copy-start(bf16[192,576]{1,0:T(8,128)(2,1)} %param.19) | copy-start | bytes 663556
  571.5 77.2 %copy-start.4 = (f32[576]{0:T(1024)S(1)}, f32[576]{0:T(1024)}, u32[]{:S(2)}) copy-start(f32[576]{0:T(1024)} %param.24) | copy-start | bytes 6916
  571.6 77.2 %copy-start.5 = (bf16[2,576]{1,0:T(2,128)(2,1)S(1)}, bf16[2,576]{1,0:T(2,128)(2,1)}, u32[]{:S(2)}) copy-start(bf16[2,576]{1,0:T(2,128)(2,1)} %param.22) | copy-start | bytes 6916
Sparse Core Ops, SparseCore 0:
  10.5 72.2 all-gather.2
  103.0 240.3 all-reduce.3
  347.8 101.0 reduce-scatter.11
  452.8 106.7 reduce-scatter.9
  571.7 58.8 reduce-scatter.13
where the time goes:
time: 658 us; the launch traced here: 657 us
  waiting for transfers between devices  292 us (44%)
  blocking collectives  227 us (34%)
  local copies, waits for them, and re-layouts  58.4 us (9%)
  matrix products  49.5 us (8%)
  between operations  14.8 us (2%)
  starting transfers between devices  8.36 us (1%)
  other arithmetic  6.68 us (1%)
    unnamed x8, waiting for transfers between devices  166 us
    unnamed x1, blocking collectives  126 us
    reduce_scatter x1, waiting for transfers between devices, body(): lax.psum_scatter(numer_all.astype(jnp.bfloat16), 'blk', scatter_dimension...  110 us
    all_gather x1, blocking collectives, body(): lax.all_gather(decode_key_value, 'blk', axis=1, tiled=True)  42.4 us
    all_gather x1, blocking collectives, body(): lax.all_gather(decode_query_rows, 'blk', axis=0, tiled=True)  42.1 us
    unnamed x43, local copies, waits for them, and re-layouts  27.1 us
    dot_general x7, matrix products, attend(): jnp.einsum('qhgk,khd->qhgd', weights.astype(jnp.bfloat16), value_rows, pr...  22.1 us
    dot_general x7, matrix products, attend(): jnp.einsum('qhgd,khd->qhgk', query_rows, key_rows, preferred_element_type...  19.9 us
  transfers between devices with their start and end apart: 9, of which 6 were waited for; matrix products, arithmetic and copies ran while one was open for 15% of the time, Pallas kernels for 0%

commit v1 on v0

--- a/solution.py
+++ b/solution.py
@@ -138,7 +138,10 @@
     )
     suffix_attn = suffix_attn.reshape(tok_rows, q_heads * head_dim)
     all_dq, all_dkv = (
-        lax.all_gather(decode_query_rows, "blk", axis=0, tiled=True),
+        jnp.concatenate(
+            lax.all_to_all(jnp.stack([decode_query_rows] * lax.axis_size("blk")), "blk", 0, 0),
+            axis=0,
+        ),
         lax.all_gather(decode_key_value, "blk", axis=1, tiled=True),
     )
     slot_total = all_dq.shape[0]

time: 658 us -> 636 us (0.967)
  blocking collectives: 227 us -> 184 us
  starting transfers between devices: 8.36 us -> 19.9 us
    all_gather x1 -> x0, blocking collectives: 42.1 us -> none  [body(): lax.all_gather(decode_query_rows, 'blk', axis=0, tiled=True)]
    all_to_all x0 -> x1, starting transfers between devices: none -> 11.6 us  [body(): lax.all_to_all(jnp.stack([decode_query_rows] * lax.axis_size('blk')), 'bl...]
    unnamed x43 -> x52, local copies, waits for them, and re-layouts: 27.1 us -> 26.1 us
  transfers between devices with their start and end apart: 9 -> 10, of which waited for: 6 -> 7; matrix products, arithmetic and copies ran while one was open for 15% -> 17% of each run, Pallas kernels for 0% -> 0%
where the time goes in v1:
time: 636 us; the launch traced here: 635 us
  waiting for transfers between devices  294 us (46%)
  blocking collectives  184 us (29%)
  local copies, waits for them, and re-layouts  62.1 us (10%)
  matrix products  52 us (8%)
  starting transfers between devices  19.9 us (3%)
  between operations  14.9 us (2%)
  other arithmetic  8.56 us (1%)
    unnamed x8, waiting for transfers between devices  169 us
    unnamed x1, blocking collectives  124 us
    reduce_scatter x1, waiting for transfers between devices, body(): lax.psum_scatter(numer_all.astype(jnp.bfloat16), 'blk', scatter_dimension...  110 us
    all_gather x1, blocking collectives, body(): lax.all_gather(decode_key_value, 'blk', axis=1, tiled=True)  43.1 us
    unnamed x52, local copies, waits for them, and re-layouts  26.1 us
    dot_general x7, matrix products, attend(): jnp.einsum('qhgk,khd->qhgd', weights.astype(jnp.bfloat16), value_rows, pr...  22.1 us
    dot_general x7, matrix products, attend(): jnp.einsum('qhgd,khd->qhgk', query_rows, key_rows, preferred_element_type...  19.9 us
    psum x1, blocking collectives, body(): mean_square = lax.psum(jnp.sum(mine * mine, axis=1), 'kv') / D  16.9 us
  transfers between devices with their start and end apart: 10, of which 7 were waited for; matrix products, arithmetic and copies ran while one was open for 17% of the time, Pallas kernels for 0%

profile of v1, /device:TPU:2, one launch (start us, length us, event | category | flops | bytes accessed | tf_op | source)
XLA Modules:
  0.0 635.1 jit_solution(5643624599501562028)
XLA Ops:
  9.2 11.6 %all-to-all-start = ((bf16[32,2,512]{2,1,0:T(2,128)(2,1)}), bf16[32,2,512]{2,1,0:T(2,128)(2,1)S(1)}, u32[]{:S(2)}, u32[]{:S(2)}) async-start(bf16[32,2,512]{2,1,0:T(2,128)(2,1)} %stack.2), calls=%async_computation.1 | async-start | bytes 131072 | tf_op jit(solution)/shard_map/all_to_all | solution.py:142
  29.1 43.1 %all_gather.7 = bf16[2,64,256]{2,0,1:T(2,128)(2,1)S(1)} all-gather(bf16[2,2,256]{2,0,1:T(2,128)(2,1)S(1)} %copy.88), channel_id=1, replica_groups=mesh['kv'=8,'blk'=32] {'blk'}, dimensions={1}, use_global_device_ids=true | all-gather | bytes 67584 | tf_op jit(solution)/shard_map/all_gather | solution.py:145
  82.9 9.7 %reshape.297 = bf16[6,1024,2,2,128]{4,3,2,1,0:T(2,128)(2,1)} reshape(bf16[6144,512]{1,0:T(8,128)(2,1)} %all-gather.2.cloned.1.call-done) | data formatting | bytes 12582912 | tf_op jit(solution)/shard_map/reshape | solution.py:115
  92.6 49.4 %while.15 = (s32[]{:T(128)}, bf16[6,1024,2,2,128]{4,1,3,2,0:T(8,128)(2,1)}, bf16[6,1024,2,2]{1,3,2,0:T(2,128)(2,1)S(1)}, s32[6,1024]{1,0:T(8,128)S(1)}, bf16[6,1...) while((s32[]{:T(128)}, ...), condition=%wide.region_6.7_spmd.clone, body=%wide.region_4.6_spmd.clone.sunk | while | flops 818278400 | bytes 19439220 | solution.py:125
  97.6 3.2 bitcast_dynamic-update-slice_fusion.4
  105.9 3.2 bitcast_dynamic-update-slice_fusion.4
  114.1 3.3 bitcast_dynamic-update-slice_fusion.4
  122.4 3.2 bitcast_dynamic-update-slice_fusion.4
  130.6 3.2 bitcast_dynamic-update-slice_fusion.4
  138.8 3.2 bitcast_dynamic-update-slice_fusion.4
  142.0 5.8 copy.117
  147.8 6.3 reshape.308
  154.2 6.1 copy.85
  164.8 7.2 %collective-permute-done = bf16[2,192,256]{2,1,0:T(8,128)(2,1)S(1)} collective-permute-done((bf16[2,192,256]{2,1,0:T(8,128)(2,1)S(1)}, bf16[2,192,256]{2,1,0:T(8,128)(2,1)S(1)}, u32[]{:S(2)}, u32[]{:S(2)}) %collective-permute-start) | collective-permute-done | bytes 196640 | tf_op jit(solution)/shard_map/ppermute | solution.py:20
  174.1 7.9 %collective-permute-done.1 = bf16[2,192,256]{2,1,0:T(8,128)(2,1)S(1)} collective-permute-done((bf16[2,192,256]{2,1,0:T(8,128)(2,1)S(1)}, bf16[2,192,256]{2,1,0:T(8,128)(2,1)S(1)}, u32[]{:S(2)}, u32[]{:S(2)}) %collective-permute-start.1) | collective-permute-done | bytes 196640 | tf_op jit(solution)/shard_map/ppermute | solution.py:20
  184.2 123.5 %all-reduce.1 = bf16[64,2,2]{2,0,1:T(8,128)(2,1)S(1)} all-reduce(bf16[64,2,2]{2,0,1:T(8,128)(2,1)S(1)} %convolution_convert_fusion.2), channel_id=5, replica_groups=mesh['kv'=8,'blk'=32] {'blk'}, use_global_device_ids=true, to_apply=%region_14.15.clone | all-reduce | flops 256 | bytes 1024
  310.0 11.7 %all-reduce.4.cloned.1.call-done = bf16[64,2,2,128]{3,0,2,1:T(8,128)(2,1)} async-done(((bf16[64,2,2,128]{3,0,2,1:T(8,128)(2,1)}), bf16[64,2,2,128]{3,0,2,1:T(8,128)(2,1)}) %all-reduce.4.cloned.1.call-update) | async-done | bytes 65552
  323.7 3.9 fusion.10
  327.6 99.7 %reduce-scatter.12.cloned.1.call-done = bf16[192,4]{1,0:T(8,128)(2,1)} async-done(((bf16[6144,4]{1,0:T(8,128)(2,1)}), bf16[192,4]{1,0:T(8,128)(2,1)}) %reduce-scatter.12.cloned.1.call-update) | async-done | bytes 1552
  428.3 109.7 %reduce-scatter.10.cloned.1.call-done = bf16[192,2,2,128]{3,0,2,1:T(8,128)(2,1)} async-done(((bf16[6144,2,2,128]{3,0,2,1:T(8,128)(2,1)}), bf16[192,2,2,128]{3,0,2,1:T(8,128)(2,1)}) %reduce-scatter.10.cloned.1.call-update) | async-done | bytes 196624 | tf_op jit(solution)/shard_map/reduce_scatter | solution.py:129
  541.2 4.7 convolution_convert_fusion
  545.9 4.0 copy.115
  552.5 56.4 %reduce-scatter.14.cloned.1.call-done = bf16[576,194]{1,0:T(8,128)(2,1)} async-done(((bf16[4608,194]{1,0:T(8,128)(2,1)}), bf16[576,194]{1,0:T(8,128)(2,1)}) %reduce-scatter.14.cloned.1.call-update) | async-done | bytes 223504
  610.2 16.9 %psum.7 = f32[194]{0:T(256)S(1)} all-reduce(f32[194]{0:T(256)S(1)} %fusion.32), channel_id=1, replica_groups=mesh['kv'=8,'blk'=32] {'kv'}, use_global_device_ids=true, to_apply=%region_17.18 | all-reduce | flops 194 | bytes 1552 | tf_op jit(solution)/shard_map/psum | solution.py:205
  (158 shorter events, 72.7 us)
Async XLA Ops:
  7.2 18.8 %copy-start = (bf16[2,16,128,256]{3,2,1,0:T(8,128)(2,1)S(1)}, bf16[2,16,128,256]{3,2,1,0:T(8,128)(2,1)}, u32[]{:S(2)}) copy-start(bf16[2,16,128,256]{3,2,1,0:T(8,128)(2,1)} %param.27) | copy-start | bytes 6291460
  7.2 75.7 %all-gather.2.cloned.1.call-start = ((), (), s32[]{:S(2)}) async-start(), calls=%async_computation.4 | async-start | bytes 6488064 | tf_op jit(solution)/shard_map/all_gather | solution.py:105
  9.2 68.0 %all-to-all-start = ((bf16[32,2,512]{2,1,0:T(2,128)(2,1)}), bf16[32,2,512]{2,1,0:T(2,128)(2,1)S(1)}, u32[]{:S(2)}, u32[]{:S(2)}) async-start(bf16[32,2,512]{2,1,0:T(2,128)(2,1)} %stack.2), calls=%async_computation.1 | async-start | bytes 131072 | tf_op jit(solution)/shard_map/all_to_all | solution.py:142
  20.9 300.8 %all-reduce.4.cloned.1.call-start = ((), (), s32[]{:S(2)}) async-start(), calls=%async_computation.8 | async-start | bytes 131072
  23.4 5.0 copy-start.15
  23.4 48.9 %copy-start.10 = (s32[512]{0:T(512)S(1)}, s32[512]{0:T(512)}, u32[]{:S(2)}) copy-start(s32[512]{0:T(512)} %param.28) | copy-start | bytes 6148
  23.4 49.1 %copy-start.16 = (s32[64]{0:T(128)S(1)}, s32[64]{0:T(128)}, u32[]{:S(2)}) copy-start(s32[64]{0:T(128)} %param.31) | copy-start | bytes 772
  72.4 4.1 copy-start.13
  82.1 10.5 %copy-start.4 = (bf16[384,2,128]{2,0,1:T(8,128)(2,1)S(1)}, bf16[384,2,128]{2,0,1:T(8,128)(2,1)}, u32[]{:S(2)}) copy-start(bf16[384,2,128]{2,0,1:T(8,128)(2,1)} %copy.84) | copy-start | bytes 589828
  82.1 10.5 %copy-start.5 = (s32[3]{0:T(128)S(1)}, s32[3]{0:T(128)}, u32[]{:S(2)}) copy-start(s32[3]{0:T(128)} %dynamic_slice.17) | copy-start | bytes 40
  82.2 345.1 %reduce-scatter.12.cloned.1.call-start = ((), (), s32[]{:S(2)}) async-start(), calls=%async_computation.6 | async-start | bytes 1622016
  154.1 383.8 %reduce-scatter.10.cloned.1.call-start = ((), (), s32[]{:S(2)}) async-start(), calls=%async_computation.5 | async-start | bytes 6488064 | tf_op jit(solution)/shard_map/reduce_scatter | solution.py:129
  160.2 3.2 copy-start.17
  160.2 4.4 copy-start.7
  160.2 4.4 copy-start.12
  160.2 23.7 %copy-start.14 = (s32[16]{0:T(128)S(1)}, s32[16]{0:T(128)}, u32[]{:S(2)}) copy-start(s32[16]{0:T(128)} %copy-done.13) | copy-start | bytes 196
  160.3 448.6 %reduce-scatter.14.cloned.1.call-start = ((), (), s32[]{:S(2)}) async-start(), calls=%async_computation.7 | async-start | bytes 2654208
  161.1 10.8 %collective-permute-start = (bf16[2,192,256]{2,1,0:T(8,128)(2,1)S(1)}, bf16[2,192,256]{2,1,0:T(8,128)(2,1)S(1)}, u32[]{:S(2)}, u32[]{:S(2)}) collective-permute-start(bf16[2,192,256]{2,1,0:T(8,128)(2,1)S(1)} %copy-done.3), channel_id=1, source_target_pairs={{0,1},{1,2},{2,3},{3,4},{4,5},{5,6},{6,7},{7,8},{8,9},{9,10},{10,1... | collective-permute-start | bytes 589832 | tf_op jit(solution)/shard_map/ppermute | solution.py:20
  171.9 10.1 %collective-permute-start.1 = (bf16[2,192,256]{2,1,0:T(8,128)(2,1)S(1)}, bf16[2,192,256]{2,1,0:T(8,128)(2,1)S(1)}, u32[]{:S(2)}, u32[]{:S(2)}) collective-permute-start(bf16[2,192,256]{2,1,0:T(8,128)(2,1)S(1)} %collective-permute-done), channel_id=1, source_target_pairs={{0,1},{1,2},{2,3},{3,4},{4,5},{5,6},{6,7},{7,8},{8,9},{9,10},{10,1... | collective-permute-start | bytes 589832 | tf_op jit(solution)/shard_map/ppermute | solution.py:20
  182.0 125.9 %collective-permute-start.2 = (bf16[2,192,256]{2,1,0:T(8,128)(2,1)S(1)}, bf16[2,192,256]{2,1,0:T(8,128)(2,1)S(1)}, u32[]{:S(2)}, u32[]{:S(2)}) collective-permute-start(bf16[2,192,256]{2,1,0:T(8,128)(2,1)S(1)} %collective-permute-done.1), channel_id=1, source_target_pairs={{0,1},{1,2},{2,3},{3,4},{4,5},{5,6},{6,7},{7,8},{8,9},{9,10},{10,1... | collective-permute-start | bytes 589832 | tf_op jit(solution)/shard_map/ppermute | solution.py:20
  307.9 14.6 %collective-permute-start.3 = (bf16[2,192,256]{2,1,0:T(8,128)(2,1)S(1)}, bf16[2,192,256]{2,1,0:T(8,128)(2,1)S(1)}, u32[]{:S(2)}, u32[]{:S(2)}) collective-permute-start(bf16[2,192,256]{2,1,0:T(8,128)(2,1)S(1)} %collective-permute-done.2), channel_id=1, source_target_pairs={{0,1},{1,2},{2,3},{3,4},{4,5},{5,6},{6,7},{7,8},{8,9},{9,10},{10,1... | collective-permute-start | bytes 589832 | tf_op jit(solution)/shard_map/ppermute | solution.py:20
  549.9 77.2 %copy-start.2 = (bf16[192,576]{1,0:T(8,128)(2,1)S(1)}, bf16[192,576]{1,0:T(8,128)(2,1)}, u32[]{:S(2)}) copy-start(bf16[192,576]{1,0:T(8,128)(2,1)} %param.19) | copy-start | bytes 663556
  549.9 77.2 %copy-start.8 = (f32[576]{0:T(1024)S(1)}, f32[576]{0:T(1024)}, u32[]{:S(2)}) copy-start(f32[576]{0:T(1024)} %param.24) | copy-start | bytes 6916
  549.9 77.2 %copy-start.9 = (bf16[2,576]{1,0:T(2,128)(2,1)S(1)}, bf16[2,576]{1,0:T(2,128)(2,1)}, u32[]{:S(2)}) copy-start(bf16[2,576]{1,0:T(2,128)(2,1)} %param.22) | copy-start | bytes 6916
  (4 other events, 8.6 us)
Sparse Core Ops, SparseCore 0:
  10.5 72.3 all-gather.1
  85.5 236.1 all-reduce.3
  326.1 101.0 reduce-scatter.11
  431.2 106.7 reduce-scatter.9
  550.1 58.8 reduce-scatter.13
